TPU v7x, 128 devices: a whole 4x4x4 slice. The times are simulated.
128 devices in a mesh: ma: 16 (over x, z), band: 8 (over y, core).
Axes of the slice: x: 4, y: 4, z: 4, core: 2. Of those that a mesh axis runs over, the one named last changes fastest.
Arguments:
- harmonics: bfloat16 [128, 8192, 256], P(('ma', 'band')), may hold values from -6 to 6
- legendre: bfloat16 [128, 2, 8192, 512], P(('ma', 'band')), may hold values from -0.0029296875 to 0.0029296875
- m_values: int32 [128], replicated, may hold values from 1 to 8191
- cycle_cell: int32 [16384], P(('ma', 'band')), may hold values from 0 to 63, as said below
- phi_cell: int32 [16384], P(('ma', 'band')), may hold values from 3 to 123
- offsets: float32 [2, 16384], P(None, ('ma', 'band')), may hold values from 0 to 1
Outputs:
- lensed: float32 [16384, 128], P(('ma', 'band'))
Inputs may be any that keep to these rules, and one draw needn't show every extreme that they name: `cycle_cell`: Band-local cycle; every point held by device (ma, band) lies in latitude band `band`. For each device and each ma index q, at most 16 of its points have cycles q * 4 to q * 4 + 3, and in every band one q receives exactly 16 points from every device of the band.
All inputs are finite; a program needn't handle non-finite values.
Results may differ from a plain program's by a relative error of at most 0.0053.
Values may be sent and summed in bfloat16 or wider, within the bound.
No kernel may reach another device: no remote copies, remote signals or barrier semaphores. Data moves between devices by JAX's collectives and lax.ppermute only.
A program may use at most 64 MiB of HBM per device.

v0:
```python
import jax
import jax.numpy as jnp
from jax import lax
from jax.sharding import PartitionSpec as P

NPHI = 128
TAPS = 8


def kernel_taps(shifts):
    return jnp.sinc(shifts) * jnp.sinc(shifts / 4.0)


def combine_parts(plus_part, minus_part):
    q_real = -(plus_part[:, 0, 0] - minus_part[:, 1, 1])
    q_imag = -(plus_part[:, 0, 1] + minus_part[:, 1, 0])
    u_real = -(plus_part[:, 1, 0] + minus_part[:, 0, 1])
    u_imag = -(plus_part[:, 1, 1] - minus_part[:, 0, 0])
    real_part = jnp.concatenate([q_real, u_real], axis=1)
    imag_part = jnp.concatenate([q_imag, u_imag], axis=1)
    return jnp.stack([real_part, imag_part], axis=1).astype(jnp.bfloat16)


def phase_table(m_values, cell_count, lmax_width):
    pixel_index = jnp.arange(cell_count, dtype=jnp.int32)
    period = 2 * lmax_width
    phase_turns = m_values[None, :] * pixel_index[:, None] % period
    angles = phase_turns.astype(jnp.float32) * (2.0 * jnp.pi / period)
    return jnp.stack([jnp.cos(angles), -jnp.sin(angles)], axis=-1).astype(jnp.bfloat16)


def spread_weights(starts, weights, length):
    tap_index = jnp.arange(TAPS, dtype=jnp.int32)
    target = starts[:, None] + tap_index[None, :]
    cells = jnp.arange(length, dtype=jnp.int32)
    hits = (target[:, :, None] == cells[None, None, :]).astype(jnp.float32)
    return jnp.sum(weights[:, :, None] * hits, axis=1)


def on_device(harmonics, legendre, m_values, cycle_cell, phi_cell, offsets):
    evolutions = harmonics.shape[2] // 4
    cycle_total = legendre.shape[3]
    owner_count = lax.axis_size("ma")
    band_count = lax.axis_size("band")
    cycle_depth = cycle_total // (owner_count * band_count)
    band_rows = owner_count * cycle_depth
    both = lax.dot_general(
        legendre[0], harmonics[0], (((1,), (0,)), ((), ())), preferred_element_type=jnp.float32
    )
    spectra = combine_parts(
        both[0].reshape(cycle_total, 2, 2, evolutions),
        both[1].reshape(cycle_total, 2, 2, evolutions),
    )
    width_out = spectra.shape[2]
    blocks = owner_count * band_count
    send = spectra.reshape(blocks, cycle_depth, 2, width_out).transpose(0, 2, 1, 3)
    received = lax.all_to_all(send, ("ma", "band"), split_axis=0, concat_axis=0, tiled=True)
    phase_rows = phase_table(m_values, NPHI, harmonics.shape[1])
    own = jnp.dot(
        phase_rows.reshape(NPHI, blocks * 2),
        received.reshape(blocks * 2, cycle_depth * width_out),
        preferred_element_type=jnp.float32,
    )
    own = (2.0 * own).astype(jnp.bfloat16).reshape(NPHI, cycle_depth, width_out)
    own = own.transpose(1, 0, 2)
    field = lax.all_gather(own, "ma", axis=0, tiled=True)
    tap_shift = jnp.arange(TAPS).astype(jnp.float32) - 3.0
    across = kernel_taps(tap_shift[None, :] - offsets[0][:, None])
    beside_all = kernel_taps(tap_shift[None, :] - offsets[1][:, None])
    cycle_weights = spread_weights(cycle_cell - 3, across, band_rows)
    phi_weights = spread_weights(phi_cell - 3, beside_all, NPHI)
    dense = (cycle_weights[:, :, None] * phi_weights[:, None, :]).astype(jnp.bfloat16)
    points = dense.shape[0]
    return jnp.dot(
        dense.reshape(points, band_rows * NPHI),
        field.reshape(band_rows * NPHI, width_out),
        preferred_element_type=jnp.float32,
    )


def solution(mesh):
    in_specs = (
        P(("ma", "band"), None, None),
        P(("ma", "band"), None, None, None),
        P(),
        P(("ma", "band")),
        P(("ma", "band")),
        P(None, ("ma", "band")),
    )
    out_specs = P(("ma", "band"), None)
    return jax.shard_map(
        on_device, mesh=mesh, in_specs=in_specs, out_specs=out_specs, check_vma=False
    )
```

profile of v0, /device:TPU:0, one launch (start us, length us, event | category | flops | bytes accessed | tf_op | source)
XLA Modules:
  0.0 93.0 jit_solution(1957809153927481940)
XLA Ops:
  6.5 9.4 %fusion = f32[2,512,256]{1,2,0:T(8,128)S(1)} fusion(bf16[1,2,8192,512]{3,2,1,0:T(8,128)(2,1)} %param.8, bf16[1,8192,256]{2,1,0:T(8,128)(2,1)} %param.7), kind=kOutput, calls=%fused_computation | convolution fusion | flops 4294967296 | bytes 22020096 | tf_op jit(solution)/shard_map/dot_general | solution.py:47
  15.9 0.1 fusion.103
  16.0 0.1 copy.58
  16.3 0.1 copy.59
  16.4 0.1 copy.60
  16.5 0.1 copy.61
  16.7 0.1 copy.62
  16.8 0.1 copy.63
  16.9 0.1 copy.64
  17.1 0.1 copy.65
  17.4 0.4 maximum_bitcast_fusion
  17.7 0.8 copy.54
  18.5 11.2 %all-to-all-start = ((bf16[128,2,4,128]{3,2,1,0:T(4,128)(2,1)}), bf16[128,2,4,128]{3,2,1,0:T(4,128)(2,1)S(1)}, u32[]{:S(2)}, u32[]{:S(2)}) async-start(bf16[128,2,4,128]{3,2,1,0:T(4,128)(2,1)} %copy.54), calls=%async_computation | async-start | bytes 524288 | tf_op jit(solution)/shard_map/all_to_all | solution.py:57
  29.8 0.3 cosine_convert_fusion
  30.1 0.1 copy.44
  30.2 10.2 %all-to-all-done = bf16[128,2,4,128]{3,2,1,0:T(4,128)(2,1)S(1)} async-done(((bf16[128,2,4,128]{3,2,1,0:T(4,128)(2,1)}), bf16[128,2,4,128]{3,2,1,0:T(4,128)(2,1)S(1)}, u32[]{:S(2)}, u32[]{:S(2)}) %all-to-all-start) | async-done | bytes 262176 | tf_op jit(solution)/shard_map/all_to_all | solution.py:57
  40.4 0.2 fusion.7
  40.7 0.7 copy.73
  41.4 0.1 fusion.41
  41.5 0.1 copy.43
  41.7 0.1 iota_add_fusion
  41.8 0.3 select_reduce_fusion
  42.1 40.5 %all-gather.2.cloned.1.call-done = bf16[64,128,128]{2,1,0:T(8,128)(2,1)} async-done(((bf16[4,128,128]{2,1,0:T(8,128)(2,1)}), bf16[64,128,128]{2,1,0:T(8,128)(2,1)}) %all-gather.2.cloned.1.call-update) | async-done | bytes 2097168 | tf_op jit(solution)/shard_map/all_gather | solution.py:66
  82.6 3.5 %fusion.8 = f32[128,128]{1,0:T(8,128)} fusion(bf16[64,128,128]{2,1,0:T(8,128)(2,1)} %all-gather.2.cloned.1.call-done, f32[128,128]{1,0:T(8,128)S(1)} %select_reduce_fusion, f32[128,64]{0,1:T(8,128)S(1)} %select_reduce_fusion.1), kind=kOutput, calls=%fused_computation.10 | convolution fusion | flops 270532608 | bytes 2260992 | tf_op jit(solution)/shard_map/dot_general | solution.py:74
  (23 shorter events, 0.4 us)
Async XLA Ops:
  16.2 13.6 %copy-start.1 = (s32[128]{0:T(128)S(1)}, s32[128]{0:T(128)}, u32[]{:S(2)}) copy-start(s32[128]{0:T(128)} %param.9) | copy-start | bytes 1540
  16.2 25.1 %copy-start = (f32[2,128]{1,0:T(2,128)S(1)}, f32[2,128]{1,0:T(2,128)}, u32[]{:S(2)}) copy-start(f32[2,128]{1,0:T(2,128)} %param.12) | copy-start | bytes 3076
  16.2 25.3 %copy-start.2 = (s32[128]{0:T(128)S(1)}, s32[128]{0:T(128)}, u32[]{:S(2)}) copy-start(s32[128]{0:T(128)} %param.10) | copy-start | bytes 1540
  16.3 25.4 %copy-start.3 = (s32[128]{0:T(128)S(1)}, s32[128]{0:T(128)}, u32[]{:S(2)}) copy-start(s32[128]{0:T(128)} %param.11) | copy-start | bytes 1540
  18.5 21.9 %all-to-all-start = ((bf16[128,2,4,128]{3,2,1,0:T(4,128)(2,1)}), bf16[128,2,4,128]{3,2,1,0:T(4,128)(2,1)S(1)}, u32[]{:S(2)}, u32[]{:S(2)}) async-start(bf16[128,2,4,128]{3,2,1,0:T(4,128)(2,1)} %copy.54), calls=%async_computation | async-start | bytes 524288 | tf_op jit(solution)/shard_map/all_to_all | solution.py:57
  29.7 52.9 %all-gather.2.cloned.1.call-start = ((), (), s32[]{:S(2)}) async-start(), calls=%async_computation.1 | async-start | bytes 2228224 | tf_op jit(solution)/shard_map/all_gather | solution.py:66
Sparse Core Ops, SparseCore 0:
  41.5 41.1 all-gather.1
where the time goes:
time: 93.2 us; the launch traced here: 93 us
  waiting for transfers between devices  50.8 us (55%)
  between operations  13.7 us (15%)
  matrix products  13.1 us (14%)
  starting transfers between devices  11.2 us (12%)
  local copies, waits for them, and re-layouts  2.87 us (3%)
  other arithmetic  1.37 us (1%)
    all_gather x1, waiting for transfers between devices, on_device(): field = lax.all_gather(own, 'ma', axis=0, tiled=True)  40.5 us
    all_to_all x1, starting transfers between devices, on_device(): lax.all_to_all(send, ('ma', 'band'), split_axis=0, concat_axis=0, tiled=T...  11.2 us
    all_to_all x1, waiting for transfers between devices, on_device(): lax.all_to_all(send, ('ma', 'band'), split_axis=0, concat_axis=0, tiled=T...  10.2 us
    dot_general x1, matrix products, on_device(): lax.dot_general(legendre[0], harmonics[0], (((1,), (0,)), ((), ())), pref...  9.38 us
    dot_general x1, matrix products, on_device(): jnp.dot(dense.reshape(points, band_rows * NPHI), field.reshape(band_rows...  3.5 us
  transfers between devices with their start and end apart: 2, of which 2 were waited for; matrix products, arithmetic and copies ran while one was open for 1% of the time, Pallas kernels for 0%

commit v1 on v0

--- a/solution.py
+++ b/solution.py
@@ -63,7 +63,9 @@
     )
     own = (2.0 * own).astype(jnp.bfloat16).reshape(NPHI, cycle_depth, width_out)
     own = own.transpose(1, 0, 2)
-    field = lax.all_gather(own, "ma", axis=0, tiled=True)
+    field = jnp.concatenate(
+        lax.all_to_all(jnp.stack([own] * lax.axis_size("ma")), "ma", 0, 0), axis=0
+    )
     tap_shift = jnp.arange(TAPS).astype(jnp.float32) - 3.0
     across = kernel_taps(tap_shift[None, :] - offsets[0][:, None])
     beside_all = kernel_taps(tap_shift[None, :] - offsets[1][:, None])

time: 93.2 us -> 74 us (0.79)
  between operations: 13.7 us -> 0.29 us
  waiting for transfers between devices: 50.8 us -> 37.4 us
  starting transfers between devices: 11.2 us -> 14.9 us
  other arithmetic: 1.37 us -> 3.7 us
  local copies, waits for them, and re-layouts: 2.87 us -> 4.18 us
    all_gather x1 -> x0, waiting for transfers between devices: 40.5 us -> none  [on_device(): field = lax.all_gather(own, 'ma', axis=0, tiled=True)]
    all_to_all x0 -> x1, waiting for transfers between devices: none -> 27.1 us  [on_device(): lax.all_to_all(jnp.stack([own] * lax.axis_size('ma')), 'ma', 0, 0)]
    all_to_all x0 -> x1, starting transfers between devices: none -> 3.72 us  [on_device(): lax.all_to_all(jnp.stack([own] * lax.axis_size('ma')), 'ma', 0, 0)]
    convert_element_type x0 -> x1, other arithmetic: none -> 2.34 us  [on_device(): (cycle_weights[:, :, None] * phi_weights[:, None, :]).astype(jnp.bfloat16)]
    another operation x0 -> x1, local copies, waits for them, and re-layouts: none -> 1.85 us  [on_device(): jnp.stack([own] * lax.axis_size('ma'))]
  transfers between devices with their start and end apart: 2 -> 2, of which waited for: 2 -> 2; matrix products, arithmetic and copies ran while one was open for 1% -> 5% of each run, Pallas kernels for 0% -> 0%
where the time goes in v1:
time: 74 us; the launch traced here: 73.7 us
  waiting for transfers between devices  37.4 us (51%)
  starting transfers between devices  14.9 us (20%)
  matrix products  13.3 us (18%)
  local copies, waits for them, and re-layouts  4.18 us (6%)
  other arithmetic  3.7 us (5%)
    all_to_all x1, waiting for transfers between devices, on_device(): lax.all_to_all(jnp.stack([own] * lax.axis_size('ma')), 'ma', 0, 0)  27.1 us
    all_to_all x1, starting transfers between devices, on_device(): lax.all_to_all(send, ('ma', 'band'), split_axis=0, concat_axis=0, tiled=T...  11.2 us
    all_to_all x1, waiting for transfers between devices, on_device(): lax.all_to_all(send, ('ma', 'band'), split_axis=0, concat_axis=0, tiled=T...  10.3 us
    dot_general x1, matrix products, on_device(): lax.dot_general(legendre[0], harmonics[0], (((1,), (0,)), ((), ())), pref...  9.39 us
    all_to_all x1, starting transfers between devices, on_device(): lax.all_to_all(jnp.stack([own] * lax.axis_size('ma')), 'ma', 0, 0)  3.72 us
    dot_general x1, matrix products, on_device(): jnp.dot(dense.reshape(points, band_rows * NPHI), field.reshape(band_rows...  3.66 us
    convert_element_type x1, other arithmetic, on_device(): (cycle_weights[:, :, None] * phi_weights[:, None, :]).astype(jnp.bfloat16)  2.34 us
    another operation x1, local copies, waits for them, and re-layouts, on_device(): jnp.stack([own] * lax.axis_size('ma'))  1.85 us
  transfers between devices with their start and end apart: 2, of which 2 were waited for; matrix products, arithmetic and copies ran while one was open for 5% of the time, Pallas kernels for 0%

profile of v1, /device:TPU:0, one launch (start us, length us, event | category | flops | bytes accessed | tf_op | source)
XLA Modules:
  0.0 73.7 jit_solution(4081525475157221817)
XLA Ops:
  0.0 9.4 %fusion = f32[2,512,256]{1,2,0:T(8,128)S(1)} fusion(bf16[1,2,8192,512]{3,2,1,0:T(8,128)(2,1)} %param.8, bf16[1,8192,256]{2,1,0:T(8,128)(2,1)} %param.7), kind=kOutput, calls=%fused_computation | convolution fusion | flops 4294967296 | bytes 22020096 | tf_op jit(solution)/shard_map/dot_general | solution.py:47
  9.5 0.1 copy.60
  9.7 0.1 copy.61
  9.8 0.1 copy.62
  10.0 0.1 copy.63
  10.1 0.1 copy.64
  10.2 0.1 copy.65
  10.4 0.1 copy.66
  10.5 0.1 copy.67
  10.8 0.4 maximum_bitcast_fusion
  11.2 0.8 %copy.56 = bf16[128,2,4,128]{3,2,1,0:T(4,128)(2,1)} copy(bf16[128,2,4,128]{3,2,0,1:T(4,128)(2,1)S(1)} %maximum_bitcast_fusion) | data formatting | bytes 524288 | tf_op jit(solution)/shard_map/transpose | solution.py:56
  12.0 11.2 %all-to-all-start = ((bf16[128,2,4,128]{3,2,1,0:T(4,128)(2,1)}), bf16[128,2,4,128]{3,2,1,0:T(4,128)(2,1)S(1)}, u32[]{:S(2)}, u32[]{:S(2)}) async-start(bf16[128,2,4,128]{3,2,1,0:T(4,128)(2,1)} %copy.56), calls=%async_computation | async-start | bytes 524288 | tf_op jit(solution)/shard_map/all_to_all | solution.py:57
  23.2 0.3 cosine_convert_fusion
  23.5 0.1 copy.46
  23.6 10.3 %all-to-all-done = bf16[128,2,4,128]{3,2,1,0:T(4,128)(2,1)S(1)} async-done(((bf16[128,2,4,128]{3,2,1,0:T(4,128)(2,1)}), bf16[128,2,4,128]{3,2,1,0:T(4,128)(2,1)S(1)}, u32[]{:S(2)}, u32[]{:S(2)}) %all-to-all-start) | async-done | bytes 262176 | tf_op jit(solution)/shard_map/all_to_all | solution.py:57
  33.9 0.2 fusion.6
  34.2 1.9 %stack.9 = bf16[16,4,128,128]{3,2,1,0:T(8,128)(2,1)} broadcast(bf16[4,128,128]{2,1,0:T(8,128)(2,1)S(1)} %copy.57), dimensions={1,2,3} | broadcast | bytes 2228224 | tf_op jit(solution)/shard_map/stack | solution.py:67
  36.0 3.7 %all-to-all-start.1 = ((bf16[16,4,128,128]{3,2,1,0:T(8,128)(2,1)}), bf16[16,4,128,128]{3,2,1,0:T(8,128)(2,1)S(1)}, u32[]{:S(2)}, u32[]{:S(2)}) async-start(bf16[16,4,128,128]{3,2,1,0:T(8,128)(2,1)} %stack.9), calls=%async_computation.1 | async-start | bytes 4194304 | tf_op jit(solution)/shard_map/all_to_all | solution.py:67
  39.8 0.1 fusion.39
  39.9 0.1 copy.45
  40.2 0.3 select_reduce_fusion
  40.6 2.3 %multiply_convert_fusion = bf16[128,64,128]{2,1,0:T(8,128)(2,1)} fusion(f32[128,128]{1,0:T(8,128)S(1)} %select_reduce_fusion, f32[128,64]{1,0:T(8,128)S(1)} %copy.44), kind=kLoop, calls=%fused_computation.3 | loop fusion | flops 2097152 | bytes 2195456 | tf_op jit(solution)/shard_map/convert_element_type | solution.py:74
  42.9 27.1 %all-to-all-done.1 = bf16[16,4,128,128]{3,2,1,0:T(8,128)(2,1)S(1)} async-done(((bf16[16,4,128,128]{3,2,1,0:T(8,128)(2,1)}), bf16[16,4,128,128]{3,2,1,0:T(8,128)(2,1)S(1)}, u32[]{:S(2)}, u32[]{:S(2)}) %all-to-all-start.1) | async-done | bytes 2097184 | tf_op jit(solution)/shard_map/all_to_all | solution.py:67
  70.1 3.7 %fusion.3 = f32[128,128]{1,0:T(8,128)} fusion(bf16[8192,128]{1,0:T(8,128)(2,1)S(1)} %bitcast.34, bf16[16,8,64,128]{3,2,1,0:T(8,128)(2,1)} %bitcast.35), kind=kOutput, calls=%fused_computation.4 | convolution fusion | flops 268435456 | bytes 4259840 | tf_op jit(solution)/shard_map/dot_general | solution.py:76
  (26 shorter events, 0.6 us)
Async XLA Ops:
  9.6 13.5 %copy-start.1 = (s32[128]{0:T(128)S(1)}, s32[128]{0:T(128)}, u32[]{:S(2)}) copy-start(s32[128]{0:T(128)} %param.9) | copy-start | bytes 1540
  12.0 27.8 %copy-start = (f32[2,128]{1,0:T(2,128)S(1)}, f32[2,128]{1,0:T(2,128)}, u32[]{:S(2)}) copy-start(f32[2,128]{1,0:T(2,128)} %param.12) | copy-start | bytes 3076
  12.0 28.0 %copy-start.2 = (s32[128]{0:T(128)S(1)}, s32[128]{0:T(128)}, u32[]{:S(2)}) copy-start(s32[128]{0:T(128)} %param.10) | copy-start | bytes 1540
  12.0 28.2 %copy-start.3 = (s32[128]{0:T(128)S(1)}, s32[128]{0:T(128)}, u32[]{:S(2)}) copy-start(s32[128]{0:T(128)} %param.11) | copy-start | bytes 1540
  12.0 21.9 %all-to-all-start = ((bf16[128,2,4,128]{3,2,1,0:T(4,128)(2,1)}), bf16[128,2,4,128]{3,2,1,0:T(4,128)(2,1)S(1)}, u32[]{:S(2)}, u32[]{:S(2)}) async-start(bf16[128,2,4,128]{3,2,1,0:T(4,128)(2,1)} %copy.56), calls=%async_computation | async-start | bytes 524288 | tf_op jit(solution)/shard_map/all_to_all | solution.py:57
  36.0 34.1 %all-to-all-start.1 = ((bf16[16,4,128,128]{3,2,1,0:T(8,128)(2,1)}), bf16[16,4,128,128]{3,2,1,0:T(8,128)(2,1)S(1)}, u32[]{:S(2)}, u32[]{:S(2)}) async-start(bf16[16,4,128,128]{3,2,1,0:T(8,128)(2,1)} %stack.9), calls=%async_computation.1 | async-start | bytes 4194304 | tf_op jit(solution)/shard_map/all_to_all | solution.py:67
